TPU v7x, 128 devices: a whole 4x4x4 slice. The times are simulated.
128 devices in a mesh: chan: 32 (over y, z, x_lo), tm: 4 (over x_hi, core).
Axes of the slice: x: 4 (x_hi: 2, x_lo: 2; x = x_hi * 2 + x_lo), y: 4, z: 4, core: 2. Of those that a mesh axis runs over, the one named last changes fastest.
Arguments:
- record: float32 [64, 256, 16384], P('tm', 'chan'), may hold values from -6 to 6
- fir_taps: float32 [64], replicated, may hold values from -0.75 to 0.75
- pair_offsets: int32 [8], replicated, may hold values from -128 to 128, as said below
Outputs:
- correlation: float32 [8, 256, 16384], P('tm', None, 'chan')
Inputs may be any that keep to these rules, and one draw needn't show every extreme that they name: `pair_offsets`: 8 distinct nonzero channel offsets; both -128 and 128 are among them.
All inputs are finite; a program needn't handle non-finite values.
Results may differ from a plain program's by a relative error of at most 0.000098.
Values sent between devices are 32-bit elements; how exact they have to be, the bound alone decides.
No kernel may reach another device: no remote copies, remote signals or barrier semaphores. Data moves between devices by JAX's collectives and lax.ppermute only.
A program may use at most 192 MiB of HBM per device.

v0:
```python
import math

import jax
import jax.numpy as jnp
from jax import lax
from jax.sharding import PartitionSpec as P

S = 256
R = 128


PRECISE = lax.Precision.HIGHEST


def extended(array, sides, width):
    for axis, dim in sides:
        size, length = (lax.axis_size(axis), array.shape[dim])
        up = [(i, (i + 1) % size) for i in range(size)]
        down = [(j, i) for i, j in up]
        last = lax.slice_in_dim(array, length - width, length, axis=dim)
        first = lax.slice_in_dim(array, 0, width, axis=dim)
        before = lax.ppermute(last, axis, up)
        after = lax.ppermute(first, axis, down)
        array = jnp.concatenate([before, array, after], axis=dim)
    return array


def fir_matrix_of(fir_taps, seg_len):
    row_ids = lax.broadcasted_iota(jnp.int32, (seg_len, seg_len), 0)
    col_ids = lax.broadcasted_iota(jnp.int32, (seg_len, seg_len), 1)
    spread = col_ids - row_ids

    def add_tap(tap_number, running):
        return running + jnp.where(spread == tap_number, fir_taps[tap_number], 0.0)

    return lax.fori_loop(0, fir_taps.shape[0], add_tap, jnp.zeros((seg_len, seg_len), jnp.float32))


def forward_table(seg_len):
    length = 2 * seg_len
    time_ids = lax.broadcasted_iota(jnp.int32, (seg_len, length), 0)
    slot_ids = lax.broadcasted_iota(jnp.int32, (seg_len, length), 1)
    frequency = jnp.where(slot_ids <= seg_len, slot_ids, slot_ids - seg_len)
    angles = (frequency * time_ids % length).astype(jnp.float32) * (2.0 * math.pi / length)
    return jnp.where(slot_ids <= seg_len, jnp.cos(angles), jnp.sin(angles))


def inverse_table(seg_len, norm_scale):
    length = 2 * seg_len
    slot_ids = lax.broadcasted_iota(jnp.int32, (3 * seg_len, seg_len), 0)
    lag_ids = lax.broadcasted_iota(jnp.int32, (3 * seg_len, seg_len), 1) - seg_len // 2
    cosine_rows = slot_ids < length
    frequency = jnp.where(
        cosine_rows, jnp.where(slot_ids <= seg_len, slot_ids, slot_ids - seg_len), slot_ids - length
    )
    angles = (frequency * lag_ids % length).astype(jnp.float32) * (2.0 * math.pi / length)
    edge_rows = (slot_ids == 0) | (slot_ids == seg_len)
    cosine_weights = jnp.where(edge_rows, 1.0 / length, 2.0 / length)
    sine_weights = jnp.where(frequency == 0, 0.0, -2.0 / length)
    values = jnp.where(
        cosine_rows, cosine_weights * jnp.cos(angles), sine_weights * jnp.sin(angles)
    )
    return values * norm_scale


def per_device(record, fir_taps, pair_offsets):
    n_chan = lax.axis_size("chan")
    n_time = lax.axis_size("tm")
    seg_count, part_rows, channels = record.shape
    block_width = channels // n_chan
    fir_matrix = fir_matrix_of(fir_taps, S)
    forward = forward_table(S)
    turned = lax.all_to_all(record, "chan", split_axis=2, concat_axis=1, tiled=True)
    widened = extended(turned, (("chan", 2),), R)
    whitened = jnp.einsum("ut,suc->stc", fir_matrix, widened, precision=PRECISE)
    spectra = jnp.einsum("stc,tj->scj", whitened, forward, precision=PRECISE)
    own_spec = spectra[:, R : R + block_width, :]
    norm_scale = 1.0 / math.sqrt(seg_count * n_time * S)
    inverse = inverse_table(S, norm_scale)
    inverse_cos = inverse[: 2 * S]
    inverse_sin = inverse[2 * S :]

    def one_offset(offset):
        partner = lax.dynamic_slice_in_dim(spectra, R + offset, block_width, axis=1)
        matched = jnp.sum(own_spec * partner, axis=0)
        skew_part = jnp.sum(
            own_spec[:, :, S:] * partner[:, :, :S] - own_spec[:, :, :S] * partner[:, :, S:], axis=0
        )
        cos_terms = jnp.einsum("rl,cr->lc", inverse_cos, matched, precision=PRECISE)
        sin_terms = jnp.einsum("rl,cr->lc", inverse_sin, skew_part, precision=PRECISE)
        return cos_terms + sin_terms

    return lax.psum_scatter(
        lax.map(one_offset, pair_offsets), "tm", scatter_dimension=0, tiled=True
    )


def solution(mesh):
    placed = (P("tm", "chan", None), P(), P())
    return jax.shard_map(
        per_device, mesh=mesh, in_specs=placed, out_specs=P("tm", None, "chan"), check_vma=False
    )
```

profile of v0, /device:TPU:1, one launch (start us, length us, event | category | flops | bytes accessed | tf_op | source)
XLA Modules:
  0.0 788.4 jit_solution(780480243956450826)
XLA Ops:
  6.5 31.7 %copy.19 = f32[16,8,16384]{0,1,2:T(8,128)} copy(f32[16,8,16384]{2,1,0:T(8,128)} %param.7) | data formatting | bytes 16777216 | tf_op args[0]
  38.2 42.6 %reshape.6 = f32[32,1,65536]{2,1,0:T(1,128)} reshape(f32[16384,8,16]{2,1,0:T(8,128)} %bitcast.21) | data formatting | bytes 16777216
  80.8 9.9 %all-to-all-start = ((f32[32,1,65536]{2,1,0:T(1,128)}), f32[32,1,65536]{2,1,0:T(1,128)}, u32[]{:S(2)}, u32[]{:S(2)}) async-start(f32[32,1,65536]{2,1,0:T(1,128)} %reshape.6), calls=%async_computation | async-start | bytes 16777216 | tf_op jit(solution)/shard_map/all_to_all | solution.py:73
  90.8 137.6 %all-to-all-done = f32[32,1,65536]{2,1,0:T(1,128)} async-done(((f32[32,1,65536]{2,1,0:T(1,128)}), f32[32,1,65536]{2,1,0:T(1,128)}, u32[]{:S(2)}, u32[]{:S(2)}) %all-to-all-start) | async-done | bytes 8388640 | tf_op jit(solution)/shard_map/all_to_all | solution.py:73
  228.9 25.1 %reduce = f32[32,65536]{1,0:T(8,128)} reduce(f32[32,1,65536]{2,1,0:T(1,128)} %all-to-all-done, f32[]{:T(128)} %broadcast.89), dimensions={1}, to_apply=%all_to_all.13.reduce_sub_computation | reduce | bytes 16777220 | tf_op jit(solution)/shard_map/all_to_all | solution.py:73
  254.1 51.3 %reshape.7 = f32[16384,8,16]{2,1,0:T(8,128)} reshape(f32[32,65536]{1,0:T(8,128)} %reduce) | data formatting | bytes 16777216
  305.4 38.3 %copy.21 = f32[16,32,8,512]{3,2,1,0:T(8,128)} copy(f32[16,32,8,512]{0,2,3,1:T(8,128)} %bitcast.6) | data formatting | bytes 16777216 | tf_op jit(solution)/shard_map/all_to_all | solution.py:73
  343.7 9.2 %copy.22 = f32[16,256,512]{1,2,0:T(8,128)} copy(f32[16,256,512]{2,1,0:T(8,128)} %bitcast.43) | data formatting | bytes 16777216 | tf_op jit(solution)/shard_map/all_to_all | solution.py:73
  352.9 4.6 fusion.42
  357.6 5.7 collective-permute-start.1
  363.3 86.0 %while.27 = (s32[]{:T(128)}, f32[256,256]{1,0:T(8,128)S(1)}, f32[64]{0:T(128)S(1)}, s32[]{:T(128)}, s32[]{:T(128)}) while((s32[]{:T(128)}, f32[256,256]{1,0:T(8,128)S(1)}, f32[64]{0:T(128)S(1)}, s32[]{:T(128)}, s32[]{:T(128)}) %tuple.66), condition=%wide.region_1.2_spmd.clone, body=%wide.region_0.1_spmd.clone.sunk | while | flops 327683 | bytes 524379 | solution.py:36
  449.3 3.4 select_multiply_fusion
  454.4 15.3 %fusion.5 = f32[16,768,256]{2,1,0:T(8,128)} fusion(f32[16,256,128]{1,2,0:T(8,128)} %collective-permute-done.1, f32[16,256,512]{1,2,0:T(8,128)} %copy.22, f32[16,256,128]{1,2,0:T(8,128)S(1)} %collective-permute-done, f32[256,256]{1,0:T(8,128)S(1)} %get-tuple-element.173), kind=kOutput, calls=%fused_computation.11 | convolution fusion | flops 9669967872 | bytes 25427968 | tf_op jit(solution)/shard_map/ut,suc->stc/dot_general | solution.py:75
  469.7 29.2 %fusion.11 = f32[16,768,512]{2,1,0:T(8,128)S(1)} fusion(f32[16,768,256]{2,1,0:T(8,128)} %fusion.5, s32[512]{0:T(512)S(1)} %iota_add_fusion.2, pred[512]{0:T(512)(128)(4,1)S(1)} %iota_compare_fusion.4), kind=kOutput, calls=%fused_computation.17 | convolution fusion | flops 19329449984 | bytes 37751296 | tf_op jit(solution)/shard_map/stc,tj->scj/dot_general | solution.py:76
  498.9 6.4 slice.46
  505.3 7.1 copy-done.1
  512.4 218.2 %while.26 = (s32[]{:T(128)}, f32[8,256,512]{2,1,0:T(8,128)}, s32[8]{0:T(128)S(1)}, f32[16,768,512]{2,1,0:T(8,128)}, f32[16,512,512]{2,1,0:T(8,128)}, /*index=5*/...) while((s32[]{:T(128)}, f32[8,256,512]{2,1,0:T(8,128)}, ...), condition=%wide.region_5.6_spmd, body=%wide.region_2.5_spmd.sunk | while | flops 1224474624 | bytes 141820656 | solution.py:94
  514.3 12.3 %fusion.59 = f32[512,256]{1,0:T(8,128)S(1)} fusion(f32[16,768,512]{2,1,0:T(8,128)} %get-tuple-element.319, s32[]{:T(128)S(6)} %select_n.128, s32[]{:T(128)S(6)} %add.122, f32[16,512,512]{2,1,0:T(8,128)} %get-tuple-element.320), kind=kLoop, calls=%fused_computation.4.clone.1 | loop fusion | flops 8257536 | bytes 34078728 | tf_op jit(solution)/shard_map/while/body/eval_jaxpr/reduce_sum | solution.py:86
  526.7 2.3 fusion.60
  528.9 1.0 copy-done
  530.0 7.7 multiply_reduce_fusion.2
  541.6 12.3 %fusion.59 = f32[512,256]{1,0:T(8,128)S(1)} fusion(f32[16,768,512]{2,1,0:T(8,128)} %get-tuple-element.319, s32[]{:T(128)S(6)} %select_n.128, s32[]{:T(128)S(6)} %add.122, f32[16,512,512]{2,1,0:T(8,128)} %get-tuple-element.320), kind=kLoop, calls=%fused_computation.4.clone.1 | loop fusion | flops 8257536 | bytes 34078728 | tf_op jit(solution)/shard_map/while/body/eval_jaxpr/reduce_sum | solution.py:86
  553.9 2.3 fusion.60
  556.2 1.0 copy-done
  557.2 7.6 multiply_reduce_fusion.2
  568.8 12.3 %fusion.59 = f32[512,256]{1,0:T(8,128)S(1)} fusion(f32[16,768,512]{2,1,0:T(8,128)} %get-tuple-element.319, s32[]{:T(128)S(6)} %select_n.128, s32[]{:T(128)S(6)} %add.122, f32[16,512,512]{2,1,0:T(8,128)} %get-tuple-element.320), kind=kLoop, calls=%fused_computation.4.clone.1 | loop fusion | flops 8257536 | bytes 34078728 | tf_op jit(solution)/shard_map/while/body/eval_jaxpr/reduce_sum | solution.py:86
  581.1 2.3 fusion.60
  584.5 7.7 multiply_reduce_fusion.2
  596.1 12.3 %fusion.59 = f32[512,256]{1,0:T(8,128)S(1)} fusion(f32[16,768,512]{2,1,0:T(8,128)} %get-tuple-element.319, s32[]{:T(128)S(6)} %select_n.128, s32[]{:T(128)S(6)} %add.122, f32[16,512,512]{2,1,0:T(8,128)} %get-tuple-element.320), kind=kLoop, calls=%fused_computation.4.clone.1 | loop fusion | flops 8257536 | bytes 34078728 | tf_op jit(solution)/shard_map/while/body/eval_jaxpr/reduce_sum | solution.py:86
  608.4 2.3 fusion.60
  610.7 1.0 copy-done
  611.8 7.7 multiply_reduce_fusion.2
  623.4 12.3 %fusion.59 = f32[512,256]{1,0:T(8,128)S(1)} fusion(f32[16,768,512]{2,1,0:T(8,128)} %get-tuple-element.319, s32[]{:T(128)S(6)} %select_n.128, s32[]{:T(128)S(6)} %add.122, f32[16,512,512]{2,1,0:T(8,128)} %get-tuple-element.320), kind=kLoop, calls=%fused_computation.4.clone.1 | loop fusion | flops 8257536 | bytes 34078728 | tf_op jit(solution)/shard_map/while/body/eval_jaxpr/reduce_sum | solution.py:86
  635.8 2.3 fusion.60
  638.0 1.0 copy-done
  639.1 7.7 multiply_reduce_fusion.2
  650.7 12.3 %fusion.59 = f32[512,256]{1,0:T(8,128)S(1)} fusion(f32[16,768,512]{2,1,0:T(8,128)} %get-tuple-element.319, s32[]{:T(128)S(6)} %select_n.128, s32[]{:T(128)S(6)} %add.122, f32[16,512,512]{2,1,0:T(8,128)} %get-tuple-element.320), kind=kLoop, calls=%fused_computation.4.clone.1 | loop fusion | flops 8257536 | bytes 34078728 | tf_op jit(solution)/shard_map/while/body/eval_jaxpr/reduce_sum | solution.py:86
  663.0 2.3 fusion.60
  666.4 7.7 multiply_reduce_fusion.2
  678.0 12.3 %fusion.59 = f32[512,256]{1,0:T(8,128)S(1)} fusion(f32[16,768,512]{2,1,0:T(8,128)} %get-tuple-element.319, s32[]{:T(128)S(6)} %select_n.128, s32[]{:T(128)S(6)} %add.122, f32[16,512,512]{2,1,0:T(8,128)} %get-tuple-element.320), kind=kLoop, calls=%fused_computation.4.clone.1 | loop fusion | flops 8257536 | bytes 34078728 | tf_op jit(solution)/shard_map/while/body/eval_jaxpr/reduce_sum | solution.py:86
  690.3 2.3 fusion.60
  692.6 1.0 copy-done
  693.7 7.7 multiply_reduce_fusion.2
  705.3 12.3 %fusion.59 = f32[512,256]{1,0:T(8,128)S(1)} fusion(f32[16,768,512]{2,1,0:T(8,128)} %get-tuple-element.319, s32[]{:T(128)S(6)} %select_n.128, s32[]{:T(128)S(6)} %add.122, f32[16,512,512]{2,1,0:T(8,128)} %get-tuple-element.320), kind=kLoop, calls=%fused_computation.4.clone.1 | loop fusion | flops 8257536 | bytes 34078728 | tf_op jit(solution)/shard_map/while/body/eval_jaxpr/reduce_sum | solution.py:86
  717.6 2.3 fusion.60
  719.9 1.0 copy-done
  720.9 7.7 multiply_reduce_fusion.2
  730.7 50.9 %reduce-scatter.2.cloned.1.call-done = f32[2,256,512]{2,1,0:T(8,128)} async-done(((f32[8,256,512]{2,1,0:T(8,128)}), f32[2,256,512]{2,1,0:T(8,128)}) %reduce-scatter.2.cloned.1.call-update) | async-done | bytes 1048592 | tf_op jit(solution)/shard_map/reduce_scatter | solution.py:93
  (194 shorter events, 109.9 us)
Async XLA Ops:
  80.8 147.6 %all-to-all-start = ((f32[32,1,65536]{2,1,0:T(1,128)}), f32[32,1,65536]{2,1,0:T(1,128)}, u32[]{:S(2)}, u32[]{:S(2)}) async-start(f32[32,1,65536]{2,1,0:T(1,128)} %reshape.6), calls=%async_computation | async-start | bytes 16777216 | tf_op jit(solution)/shard_map/all_to_all | solution.py:73
  90.8 690.8 %reduce-scatter.2.cloned.1.call-start = ((), (), s32[]{:S(2)}) async-start(), calls=%async_computation.2 | async-start | bytes 5242880 | tf_op jit(solution)/shard_map/reduce_scatter | solution.py:93
  352.9 10.3 %copy-start.3 = (f32[64]{0:T(128)S(1)}, f32[64]{0:T(128)}, u32[]{:S(2)}) copy-start(f32[64]{0:T(128)} %param.8) | copy-start | bytes 772
  357.6 96.8 %collective-permute-start = (f32[16,256,128]{1,2,0:T(8,128)}, f32[16,256,128]{1,2,0:T(8,128)S(1)}, u32[]{:S(2)}, u32[]{:S(2)}) collective-permute-start(f32[16,256,128]{1,2,0:T(8,128)} %get-tuple-element.209), channel_id=1, source_target_pairs={{0,4},{4,8},{8,12},{12,16},{16,20},{20,24},{24,28},{28,32},{32,36}... | collective-permute-start | bytes 6291464 | tf_op jit(solution)/shard_map/ppermute | solution.py:22
  357.6 96.8 %collective-permute-start.1 = (f32[16,256,128]{1,2,0:T(8,128)}, f32[16,256,128]{1,2,0:T(8,128)}, u32[]{:S(2)}, u32[]{:S(2)}) collective-permute-start(f32[16,256,128]{1,2,0:T(8,128)} %get-tuple-element.210), channel_id=1, source_target_pairs={{4,0},{8,4},{12,8},{16,12},{20,16},{24,20},{28,24},{32,28},{36,32}... | collective-permute-start | bytes 6291464 | tf_op jit(solution)/shard_map/ppermute | solution.py:23
  452.8 0.9 copy-start.2
  498.9 13.6 %copy-start.1 = (f32[16,768,512]{2,1,0:T(8,128)}, f32[16,768,512]{2,1,0:T(8,128)S(1)}, u32[]{:S(2)}) copy-start(f32[16,768,512]{2,1,0:T(8,128)S(1)} %fusion.11) | copy-start | bytes 75497472
  498.9 13.5 %slice-start = ((f32[768,256]{1,0:T(8,128)}), f32[512,256]{1,0:T(8,128)S(1)}, s32[]{:S(2)}) async-start(f32[768,256]{1,0:T(8,128)} %copy-done.2), calls=%async_computation.3 | async-start | bytes 1048576 | tf_op jit(solution)/shard_map/slice | solution.py:80
  498.9 13.5 %copy-start.4 = (s32[8]{0:T(128)S(1)}, s32[8]{0:T(128)}, u32[]{:S(2)}) copy-start(s32[8]{0:T(128)} %param.9) | copy-start | bytes 100
  514.3 15.7 %copy-start = (f32[16,512,512]{2,1,0:T(8,128)S(1)}, f32[16,512,512]{2,1,0:T(8,128)}, u32[]{:S(2)}) copy-start(f32[16,512,512]{2,1,0:T(8,128)} %get-tuple-element.320) | copy-start | bytes 50331652 | tf_op jit(solution)/shard_map/while
  541.6 15.6 %copy-start = (f32[16,512,512]{2,1,0:T(8,128)S(1)}, f32[16,512,512]{2,1,0:T(8,128)}, u32[]{:S(2)}) copy-start(f32[16,512,512]{2,1,0:T(8,128)} %get-tuple-element.320) | copy-start | bytes 50331652 | tf_op jit(solution)/shard_map/while
  568.8 15.7 %copy-start = (f32[16,512,512]{2,1,0:T(8,128)S(1)}, f32[16,512,512]{2,1,0:T(8,128)}, u32[]{:S(2)}) copy-start(f32[16,512,512]{2,1,0:T(8,128)} %get-tuple-element.320) | copy-start | bytes 50331652 | tf_op jit(solution)/shard_map/while
  596.1 15.7 %copy-start = (f32[16,512,512]{2,1,0:T(8,128)S(1)}, f32[16,512,512]{2,1,0:T(8,128)}, u32[]{:S(2)}) copy-start(f32[16,512,512]{2,1,0:T(8,128)} %get-tuple-element.320) | copy-start | bytes 50331652 | tf_op jit(solution)/shard_map/while
  623.4 15.7 %copy-start = (f32[16,512,512]{2,1,0:T(8,128)S(1)}, f32[16,512,512]{2,1,0:T(8,128)}, u32[]{:S(2)}) copy-start(f32[16,512,512]{2,1,0:T(8,128)} %get-tuple-element.320) | copy-start | bytes 50331652 | tf_op jit(solution)/shard_map/while
  650.7 15.7 %copy-start = (f32[16,512,512]{2,1,0:T(8,128)S(1)}, f32[16,512,512]{2,1,0:T(8,128)}, u32[]{:S(2)}) copy-start(f32[16,512,512]{2,1,0:T(8,128)} %get-tuple-element.320) | copy-start | bytes 50331652 | tf_op jit(solution)/shard_map/while
  678.0 15.7 %copy-start = (f32[16,512,512]{2,1,0:T(8,128)S(1)}, f32[16,512,512]{2,1,0:T(8,128)}, u32[]{:S(2)}) copy-start(f32[16,512,512]{2,1,0:T(8,128)} %get-tuple-element.320) | copy-start | bytes 50331652 | tf_op jit(solution)/shard_map/while
  705.3 15.7 %copy-start = (f32[16,512,512]{2,1,0:T(8,128)S(1)}, f32[16,512,512]{2,1,0:T(8,128)}, u32[]{:S(2)}) copy-start(f32[16,512,512]{2,1,0:T(8,128)} %get-tuple-element.320) | copy-start | bytes 50331652 | tf_op jit(solution)/shard_map/while
Sparse Core Ops, SparseCore 0:
  730.8 50.7 reduce-scatter.1
where the time goes:
time: 792 us; the launch traced here: 788 us
  local copies, waits for them, and re-layouts  252 us (32%)
  other arithmetic  236 us (30%)
  waiting for transfers between devices  189 us (24%)
  matrix products  70.6 us (9%)
  starting transfers between devices  15.7 us (2%)
  between operations  13.5 us (2%)
  loops' own time  12.1 us (2%)
    all_to_all x1, waiting for transfers between devices, per_device(): lax.all_to_all(record, 'chan', split_axis=2, concat_axis=1, tiled=True)  138 us
    unnamed x11, local copies, waits for them, and re-layouts  134 us
    reduce_sum x8, other arithmetic, one_offset(): jnp.sum(own_spec[:, :, S:] * partner[:, :, :S] - own_spec[:, :, :S] * par...  98.6 us
    reduce_sum x8, other arithmetic, one_offset(): matched = jnp.sum(own_spec * partner, axis=0)  61.4 us
    reduce_scatter x1, waiting for transfers between devices, per_device(): lax.psum_scatter(lax.map(one_offset, pair_offsets), 'tm', scatter_dimensi...  50.9 us
    all_to_all x3, local copies, waits for them, and re-layouts, per_device(): lax.all_to_all(record, 'chan', split_axis=2, concat_axis=1, tiled=True)  48 us
    add x64, other arithmetic, add_tap(): return running + jnp.where(spread == tap_number, fir_taps[tap_number], 0.0)  47.2 us
    dynamic_slice x64, local copies, waits for them, and re-layouts, add_tap(): return running + jnp.where(spread == tap_number, fir_taps[tap_number], 0.0)  37.5 us
  transfers between devices with their start and end apart: 4, of which 2 were waited for; matrix products, arithmetic and copies ran while one was open for 11% of the time, Pallas kernels for 0%

commit v1 on v0

v1 whole, which is shorter than its diff:
```python
import math

import jax
import jax.numpy as jnp
from jax import lax
from jax.sharding import PartitionSpec as P

S = 256
R = 128


PRECISE = lax.Precision.HIGHEST
FAST = lax.Precision.HIGH


def fir_matrix_of(fir_taps, seg_len):
    row_ids = lax.broadcasted_iota(jnp.int32, (seg_len, seg_len), 0)
    col_ids = lax.broadcasted_iota(jnp.int32, (seg_len, seg_len), 1)
    spread = col_ids - row_ids
    taps = fir_taps.shape[0]
    picked = jnp.take(fir_taps, jnp.clip(spread, 0, taps - 1), axis=0)
    return jnp.where((spread >= 0) & (spread < taps), picked, 0.0)


def forward_table(seg_len):
    length = 2 * seg_len
    time_ids = lax.broadcasted_iota(jnp.int32, (seg_len, length), 0)
    slot_ids = lax.broadcasted_iota(jnp.int32, (seg_len, length), 1)
    frequency = jnp.where(slot_ids <= seg_len, slot_ids, slot_ids - seg_len)
    angles = (frequency * time_ids % length).astype(jnp.float32) * (2.0 * math.pi / length)
    return jnp.where(slot_ids <= seg_len, jnp.cos(angles), jnp.sin(angles))


def inverse_table(seg_len, norm_scale):
    length = 2 * seg_len
    slot_ids = lax.broadcasted_iota(jnp.int32, (3 * seg_len, seg_len), 0)
    lag_ids = lax.broadcasted_iota(jnp.int32, (3 * seg_len, seg_len), 1) - seg_len // 2
    cosine_rows = slot_ids < length
    frequency = jnp.where(
        cosine_rows, jnp.where(slot_ids <= seg_len, slot_ids, slot_ids - seg_len), slot_ids - length
    )
    angles = (frequency * lag_ids % length).astype(jnp.float32) * (2.0 * math.pi / length)
    edge_rows = (slot_ids == 0) | (slot_ids == seg_len)
    cosine_weights = jnp.where(edge_rows, 1.0 / length, 2.0 / length)
    sine_weights = jnp.where(frequency == 0, 0.0, -2.0 / length)
    values = jnp.where(
        cosine_rows, cosine_weights * jnp.cos(angles), sine_weights * jnp.sin(angles)
    )
    return values * norm_scale


def halo(array, axis, dim, width):
    size, length = (lax.axis_size(axis), array.shape[dim])
    up = [(i, (i + 1) % size) for i in range(size)]
    down = [(j, i) for i, j in up]
    last = lax.slice_in_dim(array, length - width, length, axis=dim)
    first = lax.slice_in_dim(array, 0, width, axis=dim)
    before = lax.ppermute(last, axis, up)
    after = lax.ppermute(first, axis, down)
    return jnp.concatenate([before, array, after], axis=dim)


def per_device(record, fir_taps, pair_offsets):
    n_chan = lax.axis_size("chan")
    n_time = lax.axis_size("tm")
    seg_count, part_rows, channels = record.shape
    block_width = channels // n_chan
    table = jnp.dot(fir_matrix_of(fir_taps, S), forward_table(S), precision=PRECISE)
    table = table.reshape(n_chan, part_rows, 2 * S)
    pieces = record.reshape(seg_count, part_rows, n_chan, block_width).transpose(2, 0, 1, 3)
    turned = lax.all_to_all(pieces, "chan", split_axis=0, concat_axis=0, tiled=True)
    widened = halo(turned, "chan", 3, R)
    spectra = jnp.einsum("asuc,auj->scj", widened, table, precision=FAST)
    own_spec = spectra[:, R : R + block_width, :]
    norm_scale = 1.0 / math.sqrt(seg_count * n_time * S)
    inverse = inverse_table(S, norm_scale)
    inverse_cos = inverse[: 2 * S]
    inverse_sin = inverse[2 * S :]
    inverse_all = jnp.concatenate([inverse_cos, -inverse_sin, inverse_sin], axis=0)

    def one_offset(offset):
        partner = lax.dynamic_slice_in_dim(spectra, R + offset, block_width, axis=1)
        swapped = jnp.roll(partner, S, axis=2)
        both = jnp.concatenate([own_spec * partner, own_spec * swapped], axis=2)
        summed = jnp.sum(both, axis=0)
        return jnp.einsum("cr,rl->lc", summed, inverse_all, precision=FAST)

    even = lax.map(one_offset, pair_offsets[0::2])
    first = lax.psum_scatter(even, "tm", scatter_dimension=0, tiled=True)
    odd = lax.map(one_offset, pair_offsets[1::2])
    second = lax.psum_scatter(odd, "tm", scatter_dimension=0, tiled=True)
    return jnp.concatenate([first, second], axis=0)


def solution(mesh):
    placed = (P("tm", "chan", None), P(), P())
    return jax.shard_map(
        per_device, mesh=mesh, in_specs=placed, out_specs=P("tm", None, "chan"), check_vma=False
    )
```

time: 792 us -> 1090 us (1.38)
  local copies, waits for them, and re-layouts: 252 us -> 529 us
  other arithmetic: 236 us -> 298 us
  matrix products: 70.6 us -> 40.4 us
  waiting for transfers between devices: 189 us -> 172 us
    gather x0 -> x2, local copies, waits for them, and re-layouts: none -> 389 us  [fir_matrix_of(): picked = jnp.take(fir_taps, jnp.clip(spread, 0, taps - 1), axis=0)]
    mul x0 -> x8, other arithmetic: none -> 194 us  [one_offset(): both = jnp.concatenate([own_spec * partner, own_spec * swapped], axis=2)]
    unnamed x11 -> x12, local copies, waits for them, and re-layouts: 134 us -> 13.3 us
    slice x2 -> x11, local copies, waits for them, and re-layouts: 5.36 us -> 80.6 us  [the longest x8 77.3 us: one_offset(): swapped = jnp.roll(partner, S, axis=2)]
    reduce_sum x16 -> x8, other arithmetic: 160 us -> 97 us  [one_offset(): summed = jnp.sum(both, axis=0)]
    add x64 -> x0, other arithmetic: 47.2 us -> none  [add_tap(): return running + jnp.where(spread == tap_number, fir_taps[tap_number], 0.0)]
    all_to_all x3 -> x1, local copies, waits for them, and re-layouts: 48 us -> 9.87 us  [per_device(): lax.all_to_all(pieces, 'chan', split_axis=0, concat_axis=0, tiled=True)]
    dynamic_slice x72 -> x8, local copies, waits for them, and re-layouts: 42.2 us -> 5.05 us  [per_device(): even = lax.map(one_offset, pair_offsets[0::2])]
  transfers between devices with their start and end apart: 4 -> 5, of which waited for: 2 -> 2; matrix products, arithmetic and copies ran while one was open for 11% -> 55% of each run, Pallas kernels for 0% -> 0%
where the time goes in v1:
time: 1090 us; the launch traced here: 1080 us
  local copies, waits for them, and re-layouts  529 us (49%)
  other arithmetic  298 us (27%)
  waiting for transfers between devices  172 us (16%)
  matrix products  40.4 us (4%)
  starting transfers between devices  16 us (1%)
  between operations  13.8 us (1%)
    gather x2, local copies, waits for them, and re-layouts, fir_matrix_of(): picked = jnp.take(fir_taps, jnp.clip(spread, 0, taps - 1), axis=0)  389 us
    mul x8, other arithmetic, one_offset(): both = jnp.concatenate([own_spec * partner, own_spec * swapped], axis=2)  194 us
    all_to_all x1, waiting for transfers between devices, per_device(): lax.all_to_all(pieces, 'chan', split_axis=0, concat_axis=0, tiled=True)  133 us
    reduce_sum x8, other arithmetic, one_offset(): summed = jnp.sum(both, axis=0)  97 us
    slice x8, local copies, waits for them, and re-layouts, one_offset(): swapped = jnp.roll(partner, S, axis=2)  77.3 us
    reduce_scatter x1, waiting for transfers between devices, per_device(): second = lax.psum_scatter(odd, 'tm', scatter_dimension=0, tiled=True)  38.9 us
    dot_general x1, matrix products, per_device(): spectra = jnp.einsum('asuc,auj->scj', widened, table, precision=FAST)  29.3 us
  transfers between devices with their start and end apart: 5, of which 2 were waited for; matrix products, arithmetic and copies ran while one was open for 55% of the time, Pallas kernels for 0%

profile of v1, /device:TPU:1, one launch (start us, length us, event | category | flops | bytes accessed | tf_op | source)
XLA Modules:
  0.0 1080.1 jit_solution(13348400121929208933)
XLA Ops:
  6.5 9.9 copy.30
  16.4 8.1 copy.13
  24.5 10.3 all-to-all-start
  35.5 3.4 select_multiply_fusion
  39.2 133.2 %all-to-all-done = f32[32,16,8,512]{3,2,1,0:T(8,128)} async-done(((f32[32,16,8,512]{3,2,1,0:T(8,128)}), f32[32,16,8,512]{3,2,1,0:T(8,128)}, u32[]{:S(2)}, u32[]{:S(2)}) %all-to-all-start) | async-done | bytes 8388640 | tf_op jit(solution)/shard_map/all_to_all | solution.py:71
  172.4 9.9 copy.14
  182.3 3.2 copy-done.2
  185.5 2.5 fusion.45
  188.1 5.7 collective-permute-start.1
  193.8 389.4 %gather_fusion = f32[65536]{0:T(1024)S(1)} fusion(f32[64]{0:T(128)S(1)} %copy-done, s32[65536]{0:T(1024)S(1)} %broadcast_clamp_fusion), kind=kCustom, calls=%fused_computation | custom fusion | bytes 786432 | tf_op jit(solution)/shard_map/jit(_take)/gather | solution.py:21
  583.7 3.1 convolution_bitcast_fusion.2
  586.8 29.3 %fusion.6 = f32[16,768,512]{2,1,0:T(8,128)} fusion(f32[32,8,512,1]{2,0,1,3:T(8,128)S(1)} %convolution_bitcast_fusion.2, f32[32,16,8,128]{3,0,2,1:T(8,128)} %collective-permute-done.1, f32[32,16,8,512]{3,0,2,1:T(8,128)} %copy-done.2, f32[32,16,8,128]{3,0,2,1:T(8,128)} %collective-permute-done), kind=kOutput, calls=%fused_computation.21 | convolution fusion | flops 9669967872 | bytes 38273024 | tf_op jit(solution)/shard_map/asuc,auj->scj/dot_general | solution.py:73
  616.1 11.6 %slice.60 = f32[16,512,512]{2,1,0:T(8,128)} slice(f32[16,768,512]{2,1,0:T(8,128)} %fusion.6), slice={[0:16], [128:640], [0:512]} | slice | bytes 33554432 | tf_op jit(solution)/shard_map/slice | solution.py:74
  627.7 1.6 broadcast.125.clone2.1
  629.3 200.3 %while.24 = (s32[]{:T(128)}, f32[4,256,512]{2,1,0:T(8,128)}, s32[4]{0:T(128)S(1)}, f32[16,768,512]{2,1,0:T(8,128)}, f32[16,512,512]{2,1,0:T(8,128)}, /*index=5*/...) while((s32[]{:T(128)}, f32[4,256,512]{2,1,0:T(8,128)}, ...), condition=%wide.region_2.3_spmd, body=%wide.region_0.2_spmd.sunk | while | flops 834142208 | bytes 158859984 | solution.py:88
  631.5 9.5 constant_dynamic-slice_fusion.6
  641.0 24.3 %dynamic-slice_multiply_fusion.4 = (f32[16,512,512]{2,1,0:T(8,128)}, f32[16,512,512]{2,1,0:T(8,128)}) fusion(f32[16,512,512]{2,1,0:T(8,128)} %get-tuple-element.350, f32[16,768,512]{2,1,0:T(8,128)} %get-tuple-element.349, s32[]{:T(128)S(6)} %select_n.178, f32[16,512,256]{2,1,0:T(8,128)} %get-tuple-element.277, f32[16,512,256]{2,1,0:T(8,128)S(1)} %get-tuple-element.278), kind=kLoop, calls=%fused_computation.3.clone.1 | loop fusion | flops 12582912 | bytes 83886080 | tf_op jit(solution)/shard_map/while/body/eval_jaxpr/mul | solution.py:84
  665.3 12.1 %maximum_reduce_fusion.4 = f32[512,1024]{1,0:T(8,128)S(1)} fusion(f32[16,512,512]{2,1,0:T(8,128)} %get-tuple-element.279, f32[16,512,512]{2,1,0:T(8,128)} %get-tuple-element.280), kind=kLoop, calls=%fused_computation.1.clone.1 | loop fusion | flops 16252928 | bytes 35651584 | tf_op jit(solution)/shard_map/while/body/eval_jaxpr/reduce_sum | solution.py:85
  681.5 9.5 constant_dynamic-slice_fusion.6
  691.0 24.3 %dynamic-slice_multiply_fusion.4 = (f32[16,512,512]{2,1,0:T(8,128)}, f32[16,512,512]{2,1,0:T(8,128)}) fusion(f32[16,512,512]{2,1,0:T(8,128)} %get-tuple-element.350, f32[16,768,512]{2,1,0:T(8,128)} %get-tuple-element.349, s32[]{:T(128)S(6)} %select_n.178, f32[16,512,256]{2,1,0:T(8,128)} %get-tuple-element.277, f32[16,512,256]{2,1,0:T(8,128)S(1)} %get-tuple-element.278), kind=kLoop, calls=%fused_computation.3.clone.1 | loop fusion | flops 12582912 | bytes 83886080 | tf_op jit(solution)/shard_map/while/body/eval_jaxpr/mul | solution.py:84
  715.3 12.1 %maximum_reduce_fusion.4 = f32[512,1024]{1,0:T(8,128)S(1)} fusion(f32[16,512,512]{2,1,0:T(8,128)} %get-tuple-element.279, f32[16,512,512]{2,1,0:T(8,128)} %get-tuple-element.280), kind=kLoop, calls=%fused_computation.1.clone.1 | loop fusion | flops 16252928 | bytes 35651584 | tf_op jit(solution)/shard_map/while/body/eval_jaxpr/reduce_sum | solution.py:85
  727.4 1.0 convolution_bitcast_fusion.5
  731.5 9.5 constant_dynamic-slice_fusion.6
  741.0 24.3 %dynamic-slice_multiply_fusion.4 = (f32[16,512,512]{2,1,0:T(8,128)}, f32[16,512,512]{2,1,0:T(8,128)}) fusion(f32[16,512,512]{2,1,0:T(8,128)} %get-tuple-element.350, f32[16,768,512]{2,1,0:T(8,128)} %get-tuple-element.349, s32[]{:T(128)S(6)} %select_n.178, f32[16,512,256]{2,1,0:T(8,128)} %get-tuple-element.277, f32[16,512,256]{2,1,0:T(8,128)S(1)} %get-tuple-element.278), kind=kLoop, calls=%fused_computation.3.clone.1 | loop fusion | flops 12582912 | bytes 83886080 | tf_op jit(solution)/shard_map/while/body/eval_jaxpr/mul | solution.py:84
  765.3 12.1 %maximum_reduce_fusion.4 = f32[512,1024]{1,0:T(8,128)S(1)} fusion(f32[16,512,512]{2,1,0:T(8,128)} %get-tuple-element.279, f32[16,512,512]{2,1,0:T(8,128)} %get-tuple-element.280), kind=kLoop, calls=%fused_computation.1.clone.1 | loop fusion | flops 16252928 | bytes 35651584 | tf_op jit(solution)/shard_map/while/body/eval_jaxpr/reduce_sum | solution.py:85
  777.4 1.0 convolution_bitcast_fusion.5
  781.5 9.5 constant_dynamic-slice_fusion.6
  791.1 24.3 %dynamic-slice_multiply_fusion.4 = (f32[16,512,512]{2,1,0:T(8,128)}, f32[16,512,512]{2,1,0:T(8,128)}) fusion(f32[16,512,512]{2,1,0:T(8,128)} %get-tuple-element.350, f32[16,768,512]{2,1,0:T(8,128)} %get-tuple-element.349, s32[]{:T(128)S(6)} %select_n.178, f32[16,512,256]{2,1,0:T(8,128)} %get-tuple-element.277, f32[16,512,256]{2,1,0:T(8,128)S(1)} %get-tuple-element.278), kind=kLoop, calls=%fused_computation.3.clone.1 | loop fusion | flops 12582912 | bytes 83886080 | tf_op jit(solution)/shard_map/while/body/eval_jaxpr/mul | solution.py:84
  815.4 12.1 %maximum_reduce_fusion.4 = f32[512,1024]{1,0:T(8,128)S(1)} fusion(f32[16,512,512]{2,1,0:T(8,128)} %get-tuple-element.279, f32[16,512,512]{2,1,0:T(8,128)} %get-tuple-element.280), kind=kLoop, calls=%fused_computation.1.clone.1 | loop fusion | flops 16252928 | bytes 35651584 | tf_op jit(solution)/shard_map/while/body/eval_jaxpr/reduce_sum | solution.py:85
  829.6 1.6 broadcast.125.clone2
  831.2 200.6 %while.25 = (s32[]{:T(128)}, f32[4,256,512]{2,1,0:T(8,128)}, s32[4]{0:T(128)S(1)}, f32[16,768,512]{2,1,0:T(8,128)}, f32[16,512,512]{2,1,0:T(8,128)}, /*index=5*/...) while((s32[]{:T(128)}, f32[4,256,512]{2,1,0:T(8,128)}, ...), condition=%wide.region_6.7_spmd, body=%wide.region_4.6_spmd.sunk | while | flops 834142208 | bytes 158859984 | solution.py:90
  833.1 10.6 constant_dynamic-slice_fusion.7
  843.7 24.6 %dynamic-slice_multiply_fusion.5 = (f32[16,512,512]{2,1,0:T(8,128)}, f32[16,512,512]{2,1,0:T(8,128)}) fusion(f32[16,512,512]{2,1,0:T(8,128)} %get-tuple-element.317, f32[16,768,512]{2,1,0:T(8,128)} %get-tuple-element.316, s32[]{:T(128)S(6)} %select_n.179, f32[16,512,256]{2,1,0:T(8,128)} %get-tuple-element.287, f32[16,512,256]{2,1,0:T(8,128)S(1)} %get-tuple-element.288), kind=kLoop, calls=%fused_computation.10.clone.1 | loop fusion | flops 12582912 | bytes 83886080 | tf_op jit(solution)/shard_map/while/body/eval_jaxpr/mul | solution.py:84
  868.3 12.1 %maximum_reduce_fusion.5 = f32[512,1024]{1,0:T(8,128)S(1)} fusion(f32[16,512,512]{2,1,0:T(8,128)} %get-tuple-element.289, f32[16,512,512]{2,1,0:T(8,128)} %get-tuple-element.290), kind=kLoop, calls=%fused_computation.8.clone.1 | loop fusion | flops 16252928 | bytes 35651584 | tf_op jit(solution)/shard_map/while/body/eval_jaxpr/reduce_sum | solution.py:85
  880.4 1.0 convolution_bitcast_fusion.6
  884.3 9.5 constant_dynamic-slice_fusion.7
  893.8 24.2 %dynamic-slice_multiply_fusion.5 = (f32[16,512,512]{2,1,0:T(8,128)}, f32[16,512,512]{2,1,0:T(8,128)}) fusion(f32[16,512,512]{2,1,0:T(8,128)} %get-tuple-element.317, f32[16,768,512]{2,1,0:T(8,128)} %get-tuple-element.316, s32[]{:T(128)S(6)} %select_n.179, f32[16,512,256]{2,1,0:T(8,128)} %get-tuple-element.287, f32[16,512,256]{2,1,0:T(8,128)S(1)} %get-tuple-element.288), kind=kLoop, calls=%fused_computation.10.clone.1 | loop fusion | flops 12582912 | bytes 83886080 | tf_op jit(solution)/shard_map/while/body/eval_jaxpr/mul | solution.py:84
  918.0 12.1 %maximum_reduce_fusion.5 = f32[512,1024]{1,0:T(8,128)S(1)} fusion(f32[16,512,512]{2,1,0:T(8,128)} %get-tuple-element.289, f32[16,512,512]{2,1,0:T(8,128)} %get-tuple-element.290), kind=kLoop, calls=%fused_computation.8.clone.1 | loop fusion | flops 16252928 | bytes 35651584 | tf_op jit(solution)/shard_map/while/body/eval_jaxpr/reduce_sum | solution.py:85
  934.0 9.5 constant_dynamic-slice_fusion.7
  943.5 24.3 %dynamic-slice_multiply_fusion.5 = (f32[16,512,512]{2,1,0:T(8,128)}, f32[16,512,512]{2,1,0:T(8,128)}) fusion(f32[16,512,512]{2,1,0:T(8,128)} %get-tuple-element.317, f32[16,768,512]{2,1,0:T(8,128)} %get-tuple-element.316, s32[]{:T(128)S(6)} %select_n.179, f32[16,512,256]{2,1,0:T(8,128)} %get-tuple-element.287, f32[16,512,256]{2,1,0:T(8,128)S(1)} %get-tuple-element.288), kind=kLoop, calls=%fused_computation.10.clone.1 | loop fusion | flops 12582912 | bytes 83886080 | tf_op jit(solution)/shard_map/while/body/eval_jaxpr/mul | solution.py:84
  967.8 12.1 %maximum_reduce_fusion.5 = f32[512,1024]{1,0:T(8,128)S(1)} fusion(f32[16,512,512]{2,1,0:T(8,128)} %get-tuple-element.289, f32[16,512,512]{2,1,0:T(8,128)} %get-tuple-element.290), kind=kLoop, calls=%fused_computation.8.clone.1 | loop fusion | flops 16252928 | bytes 35651584 | tf_op jit(solution)/shard_map/while/body/eval_jaxpr/reduce_sum | solution.py:85
  979.9 1.0 convolution_bitcast_fusion.6
  983.8 9.5 constant_dynamic-slice_fusion.7
  993.4 24.3 %dynamic-slice_multiply_fusion.5 = (f32[16,512,512]{2,1,0:T(8,128)}, f32[16,512,512]{2,1,0:T(8,128)}) fusion(f32[16,512,512]{2,1,0:T(8,128)} %get-tuple-element.317, f32[16,768,512]{2,1,0:T(8,128)} %get-tuple-element.316, s32[]{:T(128)S(6)} %select_n.179, f32[16,512,256]{2,1,0:T(8,128)} %get-tuple-element.287, f32[16,512,256]{2,1,0:T(8,128)S(1)} %get-tuple-element.288), kind=kLoop, calls=%fused_computation.10.clone.1 | loop fusion | flops 12582912 | bytes 83886080 | tf_op jit(solution)/shard_map/while/body/eval_jaxpr/mul | solution.py:84
  1017.6 12.1 %maximum_reduce_fusion.5 = f32[512,1024]{1,0:T(8,128)S(1)} fusion(f32[16,512,512]{2,1,0:T(8,128)} %get-tuple-element.289, f32[16,512,512]{2,1,0:T(8,128)} %get-tuple-element.290), kind=kLoop, calls=%fused_computation.8.clone.1 | loop fusion | flops 16252928 | bytes 35651584 | tf_op jit(solution)/shard_map/while/body/eval_jaxpr/reduce_sum | solution.py:85
  1029.8 1.0 convolution_bitcast_fusion.6
  1031.9 38.9 %reduce-scatter.5.cloned.1.call-done = f32[1,256,512]{2,1,0:T(8,128)} async-done(((f32[4,256,512]{2,1,0:T(8,128)}), f32[1,256,512]{2,1,0:T(8,128)}) %reduce-scatter.5.cloned.1.call-update) | async-done | bytes 524304 | tf_op jit(solution)/shard_map/reduce_scatter | solution.py:91
  1070.8 2.2 pad_maximum_fusion.1
  (61 shorter events, 17.9 us)
Async XLA Ops:
  6.5 187.3 %copy-start = (f32[64]{0:T(128)S(1)}, f32[64]{0:T(128)}, u32[]{:S(2)}) copy-start(f32[64]{0:T(128)} %param.8) | copy-start | bytes 772
  24.5 10.3 copy-start.3
  24.5 147.9 %all-to-all-start = ((f32[32,16,8,512]{3,2,1,0:T(8,128)}), f32[32,16,8,512]{3,2,1,0:T(8,128)}, u32[]{:S(2)}, u32[]{:S(2)}) async-start(f32[32,16,8,512]{3,2,1,0:T(8,128)} %copy.13), calls=%async_computation | async-start | bytes 16777216 | tf_op jit(solution)/shard_map/all_to_all | solution.py:71
  34.8 997.1 %reduce-scatter.3.cloned.1.call-start = ((), (), s32[]{:S(2)}) async-start(), calls=%async_computation.3 | async-start | bytes 2621440 | tf_op jit(solution)/shard_map/reduce_scatter | solution.py:89
  182.3 3.2 copy-start.2
  188.1 398.7 %collective-permute-start = (f32[32,16,8,128]{3,0,2,1:T(8,128)}, f32[32,16,8,128]{3,0,2,1:T(8,128)}, u32[]{:S(2)}, u32[]{:S(2)}) collective-permute-start(f32[32,16,8,128]{3,0,2,1:T(8,128)} %get-tuple-element.193), channel_id=1, source_target_pairs={{0,4},{4,8},{8,12},{12,16},{16,20},{20,24},{24,28},{28,32},{32,36}... | collective-permute-start | bytes 6291464 | tf_op jit(solution)/shard_map/ppermute | solution.py:58
  188.1 398.7 %collective-permute-start.1 = (f32[32,16,8,128]{3,0,2,1:T(8,128)}, f32[32,16,8,128]{3,0,2,1:T(8,128)}, u32[]{:S(2)}, u32[]{:S(2)}) collective-permute-start(f32[32,16,8,128]{3,0,2,1:T(8,128)} %get-tuple-element.194), channel_id=1, source_target_pairs={{4,0},{8,4},{12,8},{16,12},{20,16},{24,20},{28,24},{32,28},{36,32}... | collective-permute-start | bytes 6291464 | tf_op jit(solution)/shard_map/ppermute | solution.py:59
  629.2 202.0 %copy-start.4 = (s32[4]{0:T(128)S(1)}, s32[4]{0:T(128)}, u32[]{:S(2)}) copy-start(s32[4]{0:T(128)} %slice.55) | copy-start | bytes 52
  829.6 241.3 %reduce-scatter.5.cloned.1.call-start = ((), (), s32[]{:S(2)}) async-start(), calls=%async_computation.4 | async-start | bytes 2621440 | tf_op jit(solution)/shard_map/reduce_scatter | solution.py:91
  1031.8 41.2 %copy-start.1 = (f32[64]{0:T(128)S(1)}, f32[64]{0:T(128)}, u32[]{:S(2)}) copy-start(f32[64]{0:T(128)} %param.8) | copy-start | bytes 772
Sparse Core Ops, SparseCore 0:
  829.7 37.3 reduce-scatter.2
  1032.0 38.8 reduce-scatter.4
